TPU v7x, 128 devices: a whole 4x4x4 slice. The times are simulated.
128 devices in a mesh: fold: 16 (over x, z), blk: 8 (over y, core).
Axes of the slice: x: 4, y: 4, z: 4, core: 2. Of those that a mesh axis runs over, the one named last changes fastest.
Arguments:
- genotypes: bfloat16 [131072, 8192], P('fold', 'blk'), may hold values from 0 to 2, as said below
- phenotypes: bfloat16 [32, 131072], P(None, 'fold'), may hold values from -4 to 4
- trait_order: int32 [32], replicated, may hold values from 0 to 31, each once
Outputs:
- predict: float32 [32, 131072], P('blk', 'fold')
Inputs may be any that keep to these rules, and one draw needn't show every extreme that they name: `genotypes`: dosages are 0, 1 or 2. `trait_order`: a permutation of the 32 traits.
All inputs are finite; a program needn't handle non-finite values.
Results may differ from a plain program's by a relative error of at most 0.00235.
Values may be sent and summed in bfloat16 or wider, within the bound.
No kernel may reach another device: no remote copies, remote signals or barrier semaphores. Data moves between devices by JAX's collectives and lax.ppermute only.
A program may use at most 320 MiB of HBM per device.

v0:
```python
import jax
import jax.numpy as jnp
from jax import lax
from jax.sharding import PartitionSpec as P

B = 512
ITERS = 8


LAMBDAS = (0.2, 2.0)
LEVEL_ONE = 0.1
EPSILON = 1e-06


def chebyshev(times_system, target, low_edge, high_edge):
    center = 0.5 * (high_edge + low_edge)
    radius = 0.5 * (high_edge - low_edge)
    sigma_ratio = center / radius
    rho_now = 1.0 / sigma_ratio
    direction = target / center
    solution = jnp.zeros_like(target)
    residual = target
    for iteration in range(ITERS):
        solution = solution + direction
        if iteration + 1 < ITERS:
            residual = residual - times_system(direction)
            rho_next = 1.0 / (2.0 * sigma_ratio - rho_now)
            direction = rho_next * rho_now * direction + 2.0 * rho_next / radius * residual
            rho_now = rho_next
    return solution


def local_gram(geno_blocks):
    return jnp.einsum("sbi,sbj->bij", geno_blocks, geno_blocks, preferred_element_type=jnp.float32)


def per_device(genotypes, phenotypes, trait_order):
    n_fold = lax.axis_size("fold")
    sample_rows = genotypes.shape[0]
    block_count = genotypes.shape[1] // B
    total_rows = sample_rows * n_fold
    held_rows = float(total_rows - sample_rows)
    geno_blocks = genotypes.reshape(sample_rows, block_count, B)
    phen = jnp.take(phenotypes, trait_order, axis=0)
    unit_row = jnp.ones((1, sample_rows), jnp.bfloat16)
    col_local = jnp.dot(unit_row, genotypes, preferred_element_type=jnp.float32).reshape(
        block_count, B
    )
    phen_local = jnp.sum(phen.astype(jnp.float32), axis=1)
    cross_local = jnp.einsum("ps,sbi->bpi", phen, geno_blocks, preferred_element_type=jnp.float32)
    col_total, phen_total = lax.psum((col_local, phen_local), "fold")
    gram_part = local_gram(geno_blocks)
    gram_sum, cross_total = lax.psum((gram_part, cross_local), "fold")
    mean_dose = col_total / total_rows
    inv_scale = 1.0 / jnp.sqrt(
        jnp.diagonal(gram_sum, axis1=1, axis2=2) / total_rows - mean_dose * mean_dose + EPSILON
    )
    gram_out = gram_sum - gram_part
    col_out = col_total - col_local
    cross_out = cross_total - cross_local
    phen_out = phen_total - phen_local
    centered = (
        gram_out
        - col_out[:, :, None] * mean_dose[:, None, :]
        - mean_dose[:, :, None] * col_out[:, None, :]
        + held_rows * mean_dose[:, :, None] * mean_dose[:, None, :]
    )
    system = inv_scale[:, :, None] * centered * inv_scale[:, None, :] / held_rows
    target = (
        (cross_out - phen_out[None, :, None] * mean_dose[:, None, :])
        * inv_scale[:, None, :]
        / held_rows
    )
    bound = jnp.max(jnp.sum(jnp.abs(system), axis=2), axis=1)
    penalty = jnp.array(LAMBDAS, jnp.float32)
    low_edge = jnp.broadcast_to(penalty[None, :, None, None], (block_count, penalty.shape[0], 1, 1))
    high_edge = low_edge + bound[:, None, None, None]

    def times_system(direction):
        return (
            jnp.einsum(
                "brpi,bij->brpj",
                direction,
                system,
                precision=lax.Precision.HIGHEST,
                preferred_element_type=jnp.float32,
            )
            + low_edge * direction
        )

    stacked = jnp.broadcast_to(target[:, None], (block_count, penalty.shape[0]) + target.shape[1:])
    coef = chebyshev(times_system, stacked, low_edge, high_edge)
    scaled = (inv_scale[:, None, None, :] * coef).astype(jnp.bfloat16)
    product = jnp.einsum("sbi,brpi->pbrs", geno_blocks, scaled, preferred_element_type=jnp.float32)
    offset = jnp.einsum(
        "bi,brpi->pbr", mean_dose, scaled.astype(jnp.float32), precision=lax.Precision.HIGHEST
    )
    feature = (product - offset[:, :, :, None]).astype(jnp.bfloat16)
    owned = lax.all_to_all(feature, "blk", split_axis=0, concat_axis=1, tiled=True)
    own_traits = owned.shape[0]
    feature_count = owned.shape[1] * owned.shape[2]
    level_feat = owned.reshape(own_traits, feature_count, sample_rows)
    target_own = lax.dynamic_slice_in_dim(phen, lax.axis_index("blk") * own_traits, own_traits, 0)
    hgram_own = jnp.einsum(
        "pqs,pts->pqt", level_feat, level_feat, preferred_element_type=jnp.float32
    )
    hcross_own = jnp.einsum(
        "pqs,ps->pq", level_feat, target_own, preferred_element_type=jnp.float32
    )
    hgram_total, hcross_total = lax.psum((hgram_own, hcross_own), "fold")
    hgram_out = hgram_total - hgram_own
    hcross_out = hcross_total - hcross_own
    trace_sum = jnp.trace(hgram_out, axis1=1, axis2=2)
    level_system = hgram_out / held_rows + (LEVEL_ONE * trace_sum / (held_rows * feature_count))[
        :, None, None
    ] * jnp.eye(feature_count, dtype=jnp.float32)
    factor = jnp.linalg.cholesky(level_system)
    weight = jax.scipy.linalg.cho_solve((factor, True), (hcross_out / held_rows)[:, :, None])[
        :, :, 0
    ]
    return jnp.einsum(
        "pq,pqs->ps", weight, level_feat.astype(jnp.float32), precision=lax.Precision.HIGHEST
    )


def solution(mesh):
    return jax.shard_map(
        per_device,
        mesh=mesh,
        in_specs=(P("fold", "blk"), P(None, "fold"), P()),
        out_specs=P("blk", "fold"),
        check_vma=False,
    )
```

profile of v0, /device:TPU:0, one launch (start us, length us, event | category | flops | bytes accessed | tf_op | source)
XLA Modules:
  0.0 373.2 jit_solution(7229157669212665997)
XLA Ops:
  6.5 0.7 compare_select_fusion
  7.3 0.7 compare_and_fusion
  7.9 18.2 %fusion.4 = f32[2,512,512]{1,2,0:T(8,128)} fusion(bf16[1024,2,8,512]{3,2,1,0:T(8,128)(2,1)} %bitcast.153), kind=kOutput, calls=%fused_computation.6 | convolution fusion | flops 8589934592 | bytes 18874368 | tf_op jit(solution)/shard_map/sbi,sbj->bij/dot_general | solution.py:34
  26.1 0.9 gather_fusion.1
  27.3 8.0 %fusion.91 = f32[2,32,512]{2,1,0:T(8,128)} fusion(bf16[1024,2,8,512]{3,2,1,0:T(8,128)(2,1)} %bitcast.154, bf16[32,8192]{1,0:T(8,128)(2,1)S(1)} %get-tuple-element.14), kind=kOutput, calls=%fused_computation.52 | convolution fusion | flops 536870912 | bytes 17432576 | tf_op jit(solution)/shard_map/ps,sbi->bpi/dot_general | solution.py:50
  35.3 28.0 %reshape.748 = bf16[8192,2,512]{2,1,0:T(2,128)(2,1)} reshape(bf16[8192,1024]{1,0:T(8,128)(2,1)} %param.4) | data formatting | bytes 33554432 | tf_op jit(solution)/shard_map/reshape | solution.py:43
  63.3 7.0 %fusion = f32[1,2,512]{2,0,1:T(1,128)S(1)} fusion(bf16[1024,2,8,512]{3,2,1,0:T(8,128)(2,1)} %bitcast.155), kind=kOutput, calls=%fused_computation.2 | convolution fusion | flops 16777216 | bytes 16781312 | tf_op jit(solution)/shard_map/dot_general | solution.py:46
  70.3 42.5 %all-reduce.1 = (f32[2,512]{1,0:T(2,128)S(1)}, f32[32]{0:T(128)S(1)}) all-reduce(f32[2,512]{1,0:T(2,128)S(1)} %bitcast.160, f32[32]{0:T(128)S(1)} %get-tuple-element.13), channel_id=1, replica_groups=mesh['fold'=16,'blk'=8] {'fold'}, use_global_device_ids=true, to_apply=%region_1.2 | all-reduce | flops 1056 | bytes 8448 | tf_op jit(solution)/shard_map/psum | solution.py:51
  112.8 16.9 %all-reduce.5.cloned.1.call-done = (f32[2,512,512]{1,2,0:T(8,128)}, f32[2,32,512]{2,1,0:T(8,128)}) async-done(((f32[2,512,512]{1,2,0:T(8,128)}, f32[2,32,512]{2,1,0:T(8,128)}), (f32[2,512,512]{1,2,0:T(8,128)}, f32[2,32,512]{2,1,0:T(8,128)})) %all-reduce.5.cloned.1.call-update) | async-done | bytes 2228240 | tf_op jit(solution)/shard_map/psum | solution.py:53
  129.7 60.1 %copy.105 = f32[2,512,512]{0,2,1:T(8,128)} copy(f32[2,512,512]{1,2,0:T(8,128)} %get-tuple-element.9) | data formatting | bytes 4194304 | tf_op jit(solution)/shard_map/psum | solution.py:53
  189.8 5.5 %gather_fusion = f32[512,2]{1,0:T(8,128)S(1)} fusion(f32[2,512,512]{0,2,1:T(8,128)} %copy.105, s32[512]{0:T(512)S(1)} %bitcast.156), kind=kCustom, calls=%fused_computation | custom fusion | bytes 12288 | tf_op jit(solution)/shard_map/jit(diagonal)/gather | solution.py:56
  195.6 3.0 abs_reduce_fusion
  198.9 2.2 fusion.37
  201.1 2.2 fusion.43
  203.3 2.2 multiply_add_fusion.2
  205.5 2.1 fusion.55
  207.7 2.2 fusion.61
  209.9 2.2 fusion.67
  212.1 2.2 fusion.88
  214.6 12.4 %fusion.17 = bf16[32,2,2,8192]{3,0,2,1:T(8,128)(2,1)S(1)} fusion(bf16[2,2,32,512]{3,2,1,0:T(8,128)(2,1)S(1)} %fusion.88, bf16[8192,2,512,1]{2,1,0,3:T(2,128)(2,1)} %bitcast.157, f32[32,2,2]{0,2,1:T(2,128)S(1)} %bitcast.164), kind=kOutput, calls=%fused_computation.15 | convolution fusion | flops 1075838976 | bytes 19005952 | tf_op jit(solution)/shard_map/sbi,brpi->pbrs/dot_general | solution.py:94
  227.0 3.5 copy.116
  230.5 4.3 %all-to-all-start = ((bf16[32,2,2,8192]{3,2,1,0:T(2,128)(2,1)}), bf16[32,2,2,8192]{3,2,1,0:T(2,128)(2,1)S(1)}, u32[]{:S(2)}, u32[]{:S(2)}) async-start(bf16[32,2,2,8192]{3,2,1,0:T(2,128)(2,1)} %copy.116), calls=%async_computation | async-start | bytes 4194304 | tf_op jit(solution)/shard_map/all_to_all | solution.py:99
  234.9 27.1 %all-to-all-done = bf16[32,2,2,8192]{3,2,1,0:T(2,128)(2,1)S(1)} async-done(((bf16[32,2,2,8192]{3,2,1,0:T(2,128)(2,1)}), bf16[32,2,2,8192]{3,2,1,0:T(2,128)(2,1)S(1)}, u32[]{:S(2)}, u32[]{:S(2)}) %all-to-all-start) | async-done | bytes 2097184 | tf_op jit(solution)/shard_map/all_to_all | solution.py:99
  262.0 3.2 copy.189
  265.1 2.7 reshape.749
  267.9 0.7 fusion.135
  268.6 0.7 fusion.99
  269.2 72.9 %all-reduce = (f32[4,32]{1,0:T(4,128)S(1)}, f32[4,32,32]{2,1,0:T(8,128)S(1)}) all-reduce(f32[4,32]{1,0:T(4,128)S(1)} %bitcast.161, f32[4,32,32]{2,1,0:T(8,128)S(1)} %fusion.135), channel_id=1, replica_groups=mesh['fold'=16,'blk'=8] {'fold'}, use_global_device_ids=true, to_apply=%region_11.12 | all-reduce | flops 4224 | bytes 33792 | tf_op jit(solution)/shard_map/psum | solution.py:110
  342.4 11.7 %custom-call.11 = f32[4,32,32]{2,1,0:T(8,128)S(1)} custom-call(f32[4,32,32]{2,1,0:T(8,128)S(1)} %fusion.115), custom_call_target="Cholesky" | custom-call | tf_op jit(solution)/shard_map/jit(cholesky)/cholesky | solution.py:117
  354.4 9.8 %custom-call.12 = f32[4,1,32,32]{2,3,1,0:T(8,128)S(1)} custom-call(f32[4,1,32,32]{3,2,1,0:T(8,128)S(1)} %select_bitcast_fusion), custom_call_target="InvertDiagBlocksLowerTriangular" | custom-call | tf_op jit(solution)/shard_map/jit(_cho_solve)/vmap()/triangular_solve | solution.py:118
  364.7 1.0 fusion.136
  365.6 0.7 copy.190
  (39 shorter events, 2.2 us)
Async XLA Ops:
  6.5 19.6 %copy-start = (bf16[32,8192]{1,0:T(8,128)(2,1)S(1)}, bf16[32,8192]{1,0:T(8,128)(2,1)}, u32[]{:S(2)}) copy-start(bf16[32,8192]{1,0:T(8,128)(2,1)} %param.5) | copy-start | bytes 1572868
  6.5 123.2 %all-reduce.5.cloned.1.call-start = ((), (), s32[]{:S(2)}) async-start(), calls=%async_computation.1 | async-start | bytes 4456448 | tf_op jit(solution)/shard_map/psum | solution.py:53
  195.5 3.2 copy-start.1
  195.5 3.2 copy-start.2
  195.5 3.3 copy-start.3
  195.6 3.3 copy-start.4
  230.5 31.5 %all-to-all-start = ((bf16[32,2,2,8192]{3,2,1,0:T(2,128)(2,1)}), bf16[32,2,2,8192]{3,2,1,0:T(2,128)(2,1)S(1)}, u32[]{:S(2)}, u32[]{:S(2)}) async-start(bf16[32,2,2,8192]{3,2,1,0:T(2,128)(2,1)} %copy.116), calls=%async_computation | async-start | bytes 4194304 | tf_op jit(solution)/shard_map/all_to_all | solution.py:99
Sparse Core Ops, SparseCore 0:
  35.5 94.1 all-reduce.4
where the time goes:
time: 375 us; the launch traced here: 373 us
  blocking collectives  115 us (31%)
  local copies, waits for them, and re-layouts  105 us (28%)
  matrix products  63.8 us (17%)
  waiting for transfers between devices  44 us (12%)
  other arithmetic  27.1 us (7%)
  between operations  13.6 us (4%)
  starting transfers between devices  4.29 us (1%)
    psum x1, blocking collectives, per_device(): hgram_total, hcross_total = lax.psum((hgram_own, hcross_own), 'fold')  72.9 us
    psum x1, local copies, waits for them, and re-layouts, per_device(): gram_sum, cross_total = lax.psum((gram_part, cross_local), 'fold')  60.1 us
    psum x1, blocking collectives, per_device(): col_total, phen_total = lax.psum((col_local, phen_local), 'fold')  42.5 us
    reshape x1, local copies, waits for them, and re-layouts, per_device(): geno_blocks = genotypes.reshape(sample_rows, block_count, B)  28 us
    all_to_all x1, waiting for transfers between devices, per_device(): lax.all_to_all(feature, 'blk', split_axis=0, concat_axis=1, tiled=True)  27.1 us
    dot_general x1, matrix products, local_gram(): jnp.einsum('sbi,sbj->bij', geno_blocks, geno_blocks, preferred_element_ty...  18.2 us
    psum x1, waiting for transfers between devices, per_device(): gram_sum, cross_total = lax.psum((gram_part, cross_local), 'fold')  16.9 us
    dot_general x7, matrix products, times_system(): jnp.einsum('brpi,bij->brpj', direction, system, precision=lax.Precision.H...  15.3 us
  transfers between devices with their start and end apart: 2, of which 2 were waited for; matrix products, arithmetic and copies ran while one was open for 9% of the time, Pallas kernels for 0%

commit v1 on v0

--- a/solution.py
+++ b/solution.py
@@ -30,8 +30,16 @@
     return solution
 
 
-def local_gram(geno_blocks):
-    return jnp.einsum("sbi,sbj->bij", geno_blocks, geno_blocks, preferred_element_type=jnp.float32)
+def butterfly_sum(x, axis):
+    n = lax.axis_size(axis)
+    if n & (n - 1):
+        return lax.psum(x, axis)
+    step = 1
+    while step < n:
+        perm = [(i, i ^ step) for i in range(n)]
+        x = x + lax.ppermute(x, axis, perm)
+        step *= 2
+    return x
 
 
 def per_device(genotypes, phenotypes, trait_order):
@@ -42,19 +50,25 @@
     held_rows = float(total_rows - sample_rows)
     geno_blocks = genotypes.reshape(sample_rows, block_count, B)
     phen = jnp.take(phenotypes, trait_order, axis=0)
-    unit_row = jnp.ones((1, sample_rows), jnp.bfloat16)
-    col_local = jnp.dot(unit_row, genotypes, preferred_element_type=jnp.float32).reshape(
-        block_count, B
-    )
+    p_size = phen.shape[0]
+    phen_aug = jnp.concatenate([phen, jnp.ones((1, sample_rows), phen.dtype)], axis=0)
+    cross_aug = jnp.dot(phen_aug, genotypes, preferred_element_type=jnp.float32)
     phen_local = jnp.sum(phen.astype(jnp.float32), axis=1)
-    cross_local = jnp.einsum("ps,sbi->bpi", phen, geno_blocks, preferred_element_type=jnp.float32)
-    col_total, phen_total = lax.psum((col_local, phen_local), "fold")
-    gram_part = local_gram(geno_blocks)
-    gram_sum, cross_total = lax.psum((gram_part, cross_local), "fold")
+    phen_row = jnp.zeros((1, genotypes.shape[1]), jnp.float32).at[0, :p_size].set(phen_local)
+    sums_local = jnp.concatenate([cross_aug, phen_row], axis=0)
+    gram_part = jnp.einsum("sbi,sbj->bij", geno_blocks, geno_blocks, preferred_element_type=jnp.float32)
+    gram_sum, sums_total = lax.psum((gram_part, sums_local), "fold")
+    phen_total = sums_total[p_size + 1, :p_size]
+    cross_aug = cross_aug.reshape(p_size + 1, block_count, B)
+    cross_aug_total = sums_total[: p_size + 1].reshape(p_size + 1, block_count, B)
+    cross_local = jnp.transpose(cross_aug[:p_size], (1, 0, 2))
+    col_local = cross_aug[p_size]
+    cross_total = jnp.transpose(cross_aug_total[:p_size], (1, 0, 2))
+    col_total = cross_aug_total[p_size]
     mean_dose = col_total / total_rows
-    inv_scale = 1.0 / jnp.sqrt(
-        jnp.diagonal(gram_sum, axis1=1, axis2=2) / total_rows - mean_dose * mean_dose + EPSILON
-    )
+    eye = jnp.eye(B, dtype=jnp.bool_)
+    gram_diag = jnp.sum(jnp.where(eye[None], gram_sum, 0.0), axis=2)
+    inv_scale = 1.0 / jnp.sqrt(gram_diag / total_rows - mean_dose * mean_dose + EPSILON)
     gram_out = gram_sum - gram_part
     col_out = col_total - col_local
     cross_out = cross_total - cross_local
@@ -91,9 +105,20 @@
     stacked = jnp.broadcast_to(target[:, None], (block_count, penalty.shape[0]) + target.shape[1:])
     coef = chebyshev(times_system, stacked, low_edge, high_edge)
     scaled = (inv_scale[:, None, None, :] * coef).astype(jnp.bfloat16)
-    product = jnp.einsum("sbi,brpi->pbrs", geno_blocks, scaled, preferred_element_type=jnp.float32)
     offset = jnp.einsum(
         "bi,brpi->pbr", mean_dose, scaled.astype(jnp.float32), precision=lax.Precision.HIGHEST
+    )
+    product = jnp.stack(
+        [
+            jnp.einsum(
+                "si,rpi->prs",
+                genotypes[:, b * B:(b + 1) * B],
+                scaled[b],
+                preferred_element_type=jnp.float32,
+            )
+            for b in range(block_count)
+        ],
+        axis=1,
     )
     feature = (product - offset[:, :, :, None]).astype(jnp.bfloat16)
     owned = lax.all_to_all(feature, "blk", split_axis=0, concat_axis=1, tiled=True)
@@ -107,7 +132,10 @@
     hcross_own = jnp.einsum(
         "pqs,ps->pq", level_feat, target_own, preferred_element_type=jnp.float32
     )
-    hgram_total, hcross_total = lax.psum((hgram_own, hcross_own), "fold")
+    level_own = jnp.concatenate([hgram_own, hcross_own[:, :, None]], axis=2)
+    level_total = butterfly_sum(level_own, "fold")
+    hgram_total = level_total[:, :, :feature_count]
+    hcross_total = level_total[:, :, feature_count]
     hgram_out = hgram_total - hgram_own
     hcross_out = hcross_total - hcross_own
     trace_sum = jnp.trace(hgram_out, axis1=1, axis2=2)

time: 375 us -> 260 us (0.69)
  blocking collectives: 115 us -> 0 us
  local copies, waits for them, and re-layouts: 105 us -> 11.6 us
  waiting for transfers between devices: 44 us -> 137 us
  matrix products: 63.8 us -> 54.3 us
  other arithmetic: 27.1 us -> 33.6 us
  starting transfers between devices: 4.29 us -> 9.79 us
    psum x2 -> x0, blocking collectives: 115 us -> none  [the longest x1 72.9 us: per_device(): hgram_total, hcross_total = lax.psum((hgram_own, hcross_own), 'fold')]
    psum x1, waiting for transfers between devices: 16.9 us -> 94.6 us  [per_device(): gram_sum, sums_total = lax.psum((gram_part, sums_local), 'fold')]
    psum x1 -> x0, local copies, waits for them, and re-layouts: 60.1 us -> none  [per_device(): gram_sum, cross_total = lax.psum((gram_part, cross_local), 'fold')]
    reshape x1 -> x0, local copies, waits for them, and re-layouts: 28 us -> none  [per_device(): geno_blocks = genotypes.reshape(sample_rows, block_count, B)]
    ppermute x0 -> x4, waiting for transfers between devices: none -> 15 us  [butterfly_sum(): x = x + lax.ppermute(x, axis, perm)]
    dot_general x4, matrix products: 45.5 us -> 36 us  [the longest x1 18.2 us: per_device(): jnp.einsum('sbi,sbj->bij', geno_blocks, geno_blocks, preferred_element_ty...]
    gather x1 -> x0, local copies, waits for them, and re-layouts: 5.54 us -> none  [per_device(): jnp.diagonal(gram_sum, axis1=1, axis2=2) / total_rows]
    ppermute x0 -> x4, starting transfers between devices: none -> 5.5 us  [butterfly_sum(): x = x + lax.ppermute(x, axis, perm)]
  transfers between devices with their start and end apart: 2 -> 6, of which waited for: 2 -> 6; matrix products, arithmetic and copies ran while one was open for 9% -> 0% of each run, Pallas kernels for 0% -> 0%
where the time goes in v1:
time: 260 us
  waiting for transfers between devices  137 us (53%)
  matrix products  54.3 us (21%)
  other arithmetic  33.6 us (13%)
  between operations  13.7 us (5%)
  local copies, waits for them, and re-layouts  11.6 us (4%)
  starting transfers between devices  9.79 us (4%)
    psum x1, waiting for transfers between devices, per_device(): gram_sum, sums_total = lax.psum((gram_part, sums_local), 'fold')  94.6 us
    all_to_all x1, waiting for transfers between devices, per_device(): lax.all_to_all(feature, 'blk', split_axis=0, concat_axis=1, tiled=True)  27.1 us
    dot_general x1, matrix products, per_device(): jnp.einsum('sbi,sbj->bij', geno_blocks, geno_blocks, preferred_element_ty...  18.2 us
    dot_general x7, matrix products, times_system(): jnp.einsum('brpi,bij->brpj', direction, system, precision=lax.Precision.H...  15.3 us
    ppermute x4, waiting for transfers between devices, butterfly_sum(): x = x + lax.ppermute(x, axis, perm)  15 us
    another operation x4, other arithmetic, per_device(): factor = jnp.linalg.cholesky(level_system)  11.9 us
    another operation x3, other arithmetic, per_device(): jax.scipy.linalg.cho_solve((factor, True), (hcross_out / held_rows)[:, :,...  9.94 us
    dot_general x2, matrix products, per_device(): jnp.einsum('si,rpi->prs', genotypes[:, b * B:(b + 1) * B], scaled[b], pre...  9.06 us
  transfers between devices with their start and end apart: 6, of which 6 were waited for; matrix products, arithmetic and copies ran while one was open for 0% of the time, Pallas kernels for 0%

profile of v1, /device:TPU:0, one launch (start us, length us, event | category | flops | bytes accessed | tf_op | source)
XLA Modules:
  0.0 259.8 jit_solution(8700191005963638330)
XLA Ops:
  8.5 0.9 gather_fusion
  9.7 8.7 %fusion.79 = f32[33,1024]{1,0:T(8,128)S(1)} fusion(bf16[8192,1024]{1,0:T(8,128)(2,1)} %param.6, bf16[32,8192]{1,0:T(8,128)(2,1)S(1)} %get-tuple-element.25), kind=kOutput, calls=%fused_computation.53 | convolution fusion | flops 553648128 | bytes 17436672 | tf_op jit(solution)/shard_map/dot_general | solution.py:55
  18.5 18.2 %fusion = f32[2,512,512]{1,2,0:T(8,128)} fusion(bf16[1024,2,8,512]{3,2,1,0:T(8,128)(2,1)} %bitcast.164), kind=kOutput, calls=%fused_computation.1 | convolution fusion | flops 8589934592 | bytes 18874368 | tf_op jit(solution)/shard_map/sbi,sbj->bij/dot_general | solution.py:59
  38.1 94.6 %all-reduce.5.cloned.1.call-done = (f32[2,512,512]{1,2,0:T(8,128)}, f32[34,1024]{1,0:T(8,128)}) async-done(((f32[2,512,512]{1,2,0:T(8,128)}, f32[34,1024]{1,0:T(8,128)}), (f32[2,512,512]{1,2,0:T(8,128)}, f32[34,1024]{1,0:T(8,128)})) %all-reduce.5.cloned.1.call-update) | async-done | bytes 2236432 | tf_op jit(solution)/shard_map/psum | solution.py:60
  134.2 0.9 slice_subtract_fusion
  135.2 2.0 select_reduce_fusion
  137.4 2.6 abs_reduce_fusion
  140.2 2.2 fusion.25
  142.4 2.2 fusion.31
  144.6 2.2 multiply_add_fusion.2
  146.8 2.1 fusion.43
  148.9 2.2 fusion.49
  151.1 2.2 fusion.55
  153.3 2.2 fusion.76
  155.5 6.4 %convolution_bitcast_fusion = f32[32,1,2,8192]{3,0,2,1:T(8,128)S(1)} fusion(bf16[8192,1024]{1,0:T(8,128)(2,1)} %param.6, bf16[2,2,32,512]{3,2,1,0:T(8,128)(2,1)S(1)} %fusion.76), kind=kOutput, calls=%fused_computation.4 | convolution fusion | flops 536870912 | bytes 10551296 | tf_op jit(solution)/shard_map/si,rpi->prs/dot_general | solution.py:113
  162.0 2.6 %convolution_bitcast_fusion.1 = f32[32,1,2,8192]{3,0,2,1:T(8,128)S(1)} fusion(bf16[8192,1024]{1,0:T(8,128)(2,1)S(1)} %bitcast.166, bf16[2,2,32,512]{3,2,1,0:T(8,128)(2,1)S(1)} %fusion.76), kind=kOutput, calls=%fused_computation.5 | convolution fusion | flops 536870912 | bytes 10551296 | tf_op jit(solution)/shard_map/si,rpi->prs/dot_general | solution.py:113
  165.4 3.5 %copy.82 = bf16[32,2,2,8192]{3,2,1,0:T(2,128)(2,1)} copy(bf16[32,2,2,8192]{3,0,2,1:T(8,128)(2,1)S(1)} %fusion.7) | data formatting | bytes 4194304 | tf_op jit(solution)/shard_map/convert_element_type | solution.py:123
  168.9 4.3 %all-to-all-start = ((bf16[32,2,2,8192]{3,2,1,0:T(2,128)(2,1)}), bf16[32,2,2,8192]{3,2,1,0:T(2,128)(2,1)S(1)}, u32[]{:S(2)}, u32[]{:S(2)}) async-start(bf16[32,2,2,8192]{3,2,1,0:T(2,128)(2,1)} %copy.82), calls=%async_computation | async-start | bytes 4194304 | tf_op jit(solution)/shard_map/all_to_all | solution.py:124
  173.2 27.1 %all-to-all-done = bf16[32,2,2,8192]{3,2,1,0:T(2,128)(2,1)S(1)} async-done(((bf16[32,2,2,8192]{3,2,1,0:T(2,128)(2,1)}), bf16[32,2,2,8192]{3,2,1,0:T(2,128)(2,1)S(1)}, u32[]{:S(2)}, u32[]{:S(2)}) %all-to-all-start) | async-done | bytes 2097184 | tf_op jit(solution)/shard_map/all_to_all | solution.py:124
  200.4 3.2 %copy.128 = bf16[8,4,2,2,8192]{4,3,2,0,1:T(2,128)(2,1)} copy(bf16[8,4,2,2,8192]{4,3,2,1,0:T(2,128)(2,1)S(1)} %bitcast.167) | data formatting | bytes 4194304 | tf_op jit(solution)/shard_map/all_to_all | solution.py:124
  203.5 2.7 %reshape.867 = bf16[4,32,8192]{2,1,0:T(8,128)(2,1)S(1)} reshape(bf16[4,8,2,2,8192]{4,3,2,1,0:T(2,128)(2,1)} %bitcast.168) | data formatting | bytes 4194304 | tf_op jit(solution)/shard_map/reshape | solution.py:127
  207.8 1.1 collective-permute-start
  209.0 3.2 %collective-permute-done = f32[4,32,33]{2,1,0:T(8,128)S(1)} collective-permute-done((f32[4,32,33]{2,1,0:T(8,128)S(1)}, f32[4,32,33]{2,1,0:T(8,128)S(1)}, u32[]{:S(2)}, u32[]{:S(2)}) %collective-permute-start) | collective-permute-done | bytes 16928 | tf_op jit(solution)/shard_map/ppermute | solution.py:40
  212.3 1.8 collective-permute-start.1
  214.1 4.1 %collective-permute-done.1 = f32[4,32,33]{2,1,0:T(8,128)S(1)} collective-permute-done((f32[4,32,33]{2,1,0:T(8,128)S(1)}, f32[4,32,33]{2,1,0:T(8,128)S(1)}, u32[]{:S(2)}, u32[]{:S(2)}) %collective-permute-start.1) | collective-permute-done | bytes 16928 | tf_op jit(solution)/shard_map/ppermute | solution.py:40
  218.1 0.9 collective-permute-start.2
  219.1 3.5 %collective-permute-done.2 = f32[4,32,33]{2,1,0:T(8,128)S(1)} collective-permute-done((f32[4,32,33]{2,1,0:T(8,128)S(1)}, f32[4,32,33]{2,1,0:T(8,128)S(1)}, u32[]{:S(2)}, u32[]{:S(2)}) %collective-permute-start.2) | collective-permute-done | bytes 16928 | tf_op jit(solution)/shard_map/ppermute | solution.py:40
  222.6 1.6 collective-permute-start.3
  224.3 4.2 %collective-permute-done.3 = f32[4,32,33]{2,1,0:T(8,128)S(1)} collective-permute-done((f32[4,32,33]{2,1,0:T(8,128)S(1)}, f32[4,32,33]{2,1,0:T(8,128)S(1)}, u32[]{:S(2)}, u32[]{:S(2)}) %collective-permute-start.3) | collective-permute-done | bytes 16928 | tf_op jit(solution)/shard_map/ppermute | solution.py:40
  229.0 11.7 %custom-call.11 = f32[4,32,32]{2,1,0:T(8,128)S(1)} custom-call(f32[4,32,32]{2,1,0:T(8,128)S(1)} %fusion.104), custom_call_target="Cholesky" | custom-call | tf_op jit(solution)/shard_map/jit(cholesky)/cholesky | solution.py:145
  241.0 9.8 %custom-call.12 = f32[4,1,32,32]{2,3,1,0:T(8,128)S(1)} custom-call(f32[4,1,32,32]{3,2,1,0:T(8,128)S(1)} %select_bitcast_fusion), custom_call_target="InvertDiagBlocksLowerTriangular" | custom-call | tf_op jit(solution)/shard_map/jit(_cho_solve)/vmap()/triangular_solve | solution.py:146
  251.2 1.0 fusion.123
  (63 shorter events, 10.0 us)
Async XLA Ops:
  6.5 2.0 copy-start
  6.5 126.2 %all-reduce.5.cloned.1.call-start = ((), (), s32[]{:S(2)}) async-start(), calls=%async_computation.1 | async-start | bytes 4521984 | tf_op jit(solution)/shard_map/psum | solution.py:60
  135.2 2.2 copy-start.1
  137.4 2.7 %copy-start.2 = (f32[2]{0:T(128)S(1)}, f32[2]{0:T(128)}, u32[]{:S(2)}) copy-start(f32[2]{0:T(128)} %constant.144.clone) | copy-start | bytes 28
  137.4 2.7 %copy-start.3 = (f32[2]{0:T(128)S(1)}, f32[2]{0:T(128)}, u32[]{:S(2)}) copy-start(f32[2]{0:T(128)} %constant.149) | copy-start | bytes 28
  140.2 21.8 %slice-start = ((s8[16777216]{0:T(1024)(128)(4,1)}), s8[4194304]{0:T(1024)(128)(4,1)S(1)}, s32[]{:S(2)}) async-start(s8[16777216]{0:T(1024)(128)(4,1)} %bitcast.165), calls=%async_computation.2 | async-start | bytes 8388608
  144.6 17.4 %slice-start.1 = ((s8[16777216]{0:T(1024)(128)(4,1)}), s8[4194304]{0:T(1024)(128)(4,1)S(1)}, s32[]{:S(2)}) async-start(s8[16777216]{0:T(1024)(128)(4,1)} %bitcast.165), calls=%async_computation.3 | async-start | bytes 8388608
  151.1 10.8 %slice-start.2 = ((s8[16777216]{0:T(1024)(128)(4,1)}), s8[4194304]{0:T(1024)(128)(4,1)S(1)}, s32[]{:S(2)}) async-start(s8[16777216]{0:T(1024)(128)(4,1)} %bitcast.165), calls=%async_computation.4 | async-start | bytes 8388608
  155.5 6.5 %slice-start.3 = ((s8[16777216]{0:T(1024)(128)(4,1)}), s8[4194304]{0:T(1024)(128)(4,1)S(1)}, s32[]{:S(2)}) async-start(s8[16777216]{0:T(1024)(128)(4,1)} %bitcast.165), calls=%async_computation.5 | async-start | bytes 8388608
  168.9 31.5 %all-to-all-start = ((bf16[32,2,2,8192]{3,2,1,0:T(2,128)(2,1)}), bf16[32,2,2,8192]{3,2,1,0:T(2,128)(2,1)S(1)}, u32[]{:S(2)}, u32[]{:S(2)}) async-start(bf16[32,2,2,8192]{3,2,1,0:T(2,128)(2,1)} %copy.82), calls=%async_computation | async-start | bytes 4194304 | tf_op jit(solution)/shard_map/all_to_all | solution.py:124
  207.8 4.3 %collective-permute-start = (f32[4,32,33]{2,1,0:T(8,128)S(1)}, f32[4,32,33]{2,1,0:T(8,128)S(1)}, u32[]{:S(2)}, u32[]{:S(2)}) collective-permute-start(f32[4,32,33]{2,1,0:T(8,128)S(1)} %pad_maximum_fusion), channel_id=1, source_target_pairs={{0,8},{8,0},{16,24},{24,16},{32,40},{40,32},{48,56},{56,48},{64,72... | collective-permute-start | bytes 50696 | tf_op jit(solution)/shard_map/ppermute | solution.py:40
  212.3 5.8 %collective-permute-start.1 = (f32[4,32,33]{2,1,0:T(8,128)S(1)}, f32[4,32,33]{2,1,0:T(8,128)S(1)}, u32[]{:S(2)}, u32[]{:S(2)}) collective-permute-start(f32[4,32,33]{2,1,0:T(8,128)S(1)} %fusion.135), channel_id=1, source_target_pairs={{0,16},{8,24},{16,0},{24,8},{32,48},{40,56},{48,32},{56,40},{64,80... | collective-permute-start | bytes 50696 | tf_op jit(solution)/shard_map/ppermute | solution.py:40
  218.1 4.5 %collective-permute-start.2 = (f32[4,32,33]{2,1,0:T(8,128)S(1)}, f32[4,32,33]{2,1,0:T(8,128)S(1)}, u32[]{:S(2)}, u32[]{:S(2)}) collective-permute-start(f32[4,32,33]{2,1,0:T(8,128)S(1)} %add.271), channel_id=1, source_target_pairs={{0,32},{8,40},{16,48},{24,56},{32,0},{40,8},{48,16},{56,24},{64,96... | collective-permute-start | bytes 50696 | tf_op jit(solution)/shard_map/ppermute | solution.py:40
  222.6 5.8 %collective-permute-start.3 = (f32[4,32,33]{2,1,0:T(8,128)S(1)}, f32[4,32,33]{2,1,0:T(8,128)S(1)}, u32[]{:S(2)}, u32[]{:S(2)}) collective-permute-start(f32[4,32,33]{2,1,0:T(8,128)S(1)} %add.272), channel_id=1, source_target_pairs={{0,64},{8,72},{16,80},{24,88},{32,96},{40,104},{48,112},{56,120},{... | collective-permute-start | bytes 50696 | tf_op jit(solution)/shard_map/ppermute | solution.py:40
Sparse Core Ops, SparseCore 0:
  38.1 94.5 all-reduce.4

commit v2 on v1

--- a/solution.py
+++ b/solution.py
@@ -48,16 +48,51 @@
     block_count = genotypes.shape[1] // B
     total_rows = sample_rows * n_fold
     held_rows = float(total_rows - sample_rows)
-    geno_blocks = genotypes.reshape(sample_rows, block_count, B)
     phen = jnp.take(phenotypes, trait_order, axis=0)
     p_size = phen.shape[0]
+    half = B // 2
+    rows = lax.broadcasted_iota(jnp.int32, (half, half), 0)
+    cols = lax.broadcasted_iota(jnp.int32, (half, half), 1)
+    eye_h = rows == cols
+
+    def pack(gram):
+        a11, a12, a22 = gram[:half, :half], gram[:half, half:], gram[half:, half:]
+        tile = jnp.where(rows > cols, a11, a22)
+        diag = jnp.sum(jnp.where(eye_h, a11, 0.0), axis=1)
+        return jnp.concatenate([a12, tile, diag[None]], axis=0)
+
+    def unpack(packed):
+        a12, tile, diag = packed[:half], packed[half:B], packed[B]
+        tile_t = tile.T
+        a22 = jnp.where(rows <= cols, tile, tile_t)
+        a11 = jnp.where(rows > cols, tile, jnp.where(rows < cols, tile_t, jnp.where(eye_h, diag[:, None], 0.0)))
+        top = jnp.concatenate([a11, a12], axis=1)
+        bottom = jnp.concatenate([a12.T, a22], axis=1)
+        return jnp.concatenate([top, bottom], axis=0)
+
+    gram_parts = []
+    packed_sums = []
+    for b in range(block_count):
+        xb = genotypes[:, b * B:(b + 1) * B]
+        gram_b = jnp.einsum("si,sj->ij", xb, xb, preferred_element_type=jnp.float32)
+        gram_parts.append(gram_b)
+        if b + 1 < block_count:
+            packed = pack(gram_b)
+            if packed_sums:
+                packed = packed.at[0, 0].add(packed_sums[-1][0, 0] * 0.0)
+            packed_sums.append(lax.psum(packed, "fold"))
     phen_aug = jnp.concatenate([phen, jnp.ones((1, sample_rows), phen.dtype)], axis=0)
     cross_aug = jnp.dot(phen_aug, genotypes, preferred_element_type=jnp.float32)
     phen_local = jnp.sum(phen.astype(jnp.float32), axis=1)
     phen_row = jnp.zeros((1, genotypes.shape[1]), jnp.float32).at[0, :p_size].set(phen_local)
     sums_local = jnp.concatenate([cross_aug, phen_row], axis=0)
-    gram_part = jnp.einsum("sbi,sbj->bij", geno_blocks, geno_blocks, preferred_element_type=jnp.float32)
-    gram_sum, sums_total = lax.psum((gram_part, sums_local), "fold")
+    last_packed = pack(gram_parts[-1])
+    if packed_sums:
+        last_packed = last_packed.at[0, 0].add(packed_sums[-1][0, 0] * 0.0)
+    last_packed, sums_total = lax.psum((last_packed, sums_local), "fold")
+    packed_sums.append(last_packed)
+    gram_part = jnp.stack(gram_parts)
+    gram_sum = jnp.stack([unpack(p) for p in packed_sums])
     phen_total = sums_total[p_size + 1, :p_size]
     cross_aug = cross_aug.reshape(p_size + 1, block_count, B)
     cross_aug_total = sums_total[: p_size + 1].reshape(p_size + 1, block_count, B)

time: 260 us -> 324 us (1.25)
  waiting for transfers between devices: 137 us -> 184 us
  local copies, waits for them, and re-layouts: 11.6 us -> 26 us
  other arithmetic: 33.6 us -> 37.6 us
  matrix products: 54.3 us -> 50.9 us
    psum x1 -> x2, waiting for transfers between devices: 94.6 us -> 142 us  [the longest x1 78.6 us: per_device(): last_packed, sums_total = lax.psum((last_packed, sums_local), 'fold')]
    slice x0 -> x10, local copies, waits for them, and re-layouts: none -> 5.87 us  [the longest x7 4.43 us: unpack(): a12, tile, diag = (packed[:half], packed[half:B], packed[B])]
    dot_general x7, matrix products: 15.3 us -> 10.3 us  [times_system(): jnp.einsum('brpi,bij->brpj', direction, system, precision=lax.Precision.H...]
    dot_general x1 -> x2, matrix products: 18.2 us -> 19.9 us  [per_device(): gram_b = jnp.einsum('si,sj->ij', xb, xb, preferred_element_type=jnp.float32)]
  transfers between devices with their start and end apart: 6 -> 7, of which waited for: 6 -> 7; matrix products, arithmetic and copies ran while one was open for 0% -> 9% of each run, Pallas kernels for 0% -> 0%
where the time goes in v2:
time: 324 us
  waiting for transfers between devices  184 us (57%)
  matrix products  50.9 us (16%)
  other arithmetic  37.6 us (12%)
  local copies, waits for them, and re-layouts  26 us (8%)
  between operations  15.4 us (5%)
  starting transfers between devices  10.2 us (3%)
    psum x1, waiting for transfers between devices, per_device(): last_packed, sums_total = lax.psum((last_packed, sums_local), 'fold')  78.6 us
    psum x1, waiting for transfers between devices, per_device(): packed_sums.append(lax.psum(packed, 'fold'))  63.2 us
    all_to_all x1, waiting for transfers between devices, per_device(): lax.all_to_all(feature, 'blk', split_axis=0, concat_axis=1, tiled=True)  27.1 us
    dot_general x2, matrix products, per_device(): gram_b = jnp.einsum('si,sj->ij', xb, xb, preferred_element_type=jnp.float32)  19.9 us
    ppermute x4, waiting for transfers between devices, butterfly_sum(): x = x + lax.ppermute(x, axis, perm)  14.8 us
    another operation x4, other arithmetic, per_device(): factor = jnp.linalg.cholesky(level_system)  11.9 us
    dot_general x7, matrix products, times_system(): jnp.einsum('brpi,bij->brpj', direction, system, precision=lax.Precision.H...  10.3 us
    another operation x3, other arithmetic, per_device(): jax.scipy.linalg.cho_solve((factor, True), (hcross_out / held_rows)[:, :,...  9.94 us
  transfers between devices with their start and end apart: 7, of which 7 were waited for; matrix products, arithmetic and copies ran while one was open for 9% of the time, Pallas kernels for 0%

profile of v2, /device:TPU:0, one launch (start us, length us, event | category | flops | bytes accessed | tf_op | source)
XLA Modules:
  0.0 323.8 jit_solution(1646531257108020999)
XLA Ops:
  6.5 9.9 %fusion.6 = f32[512,512]{1,0:T(8,128)S(1)} fusion(bf16[8192,1024]{1,0:T(8,128)(2,1)} %param.8), kind=kOutput, calls=%fused_computation.9 | convolution fusion | flops 4294967296 | bytes 9437184 | tf_op jit(solution)/shard_map/si,sj->ij/dot_general | solution.py:77
  20.0 10.0 %fusion.3 = f32[512,512]{1,0:T(8,128)S(1)} fusion(bf16[8192,1024]{1,0:T(8,128)(2,1)} %param.8), kind=kOutput, calls=%fused_computation.6 | convolution fusion | flops 4294967296 | bytes 9437184 | tf_op jit(solution)/shard_map/si,sj->ij/dot_general | solution.py:77
  32.3 8.8 %fusion.86 = f32[33,1024]{1,0:T(8,128)S(1)} fusion(bf16[8192,1024]{1,0:T(8,128)(2,1)} %param.8, bf16[32,8192]{1,0:T(8,128)(2,1)S(1)} %get-tuple-element.37), kind=kOutput, calls=%fused_computation.65 | convolution fusion | flops 553648128 | bytes 17436672 | tf_op jit(solution)/shard_map/dot_general | solution.py:85
  44.2 63.2 %all-reduce.6.cloned.1.call-done = f32[513,256]{1,0:T(8,128)} async-done(((f32[513,256]{1,0:T(8,128)}), f32[513,256]{1,0:T(8,128)}) %all-reduce.6.cloned.1.call-update) | async-done | bytes 525328 | tf_op jit(solution)/shard_map/psum | solution.py:83
  112.8 1.8 fusion.136
  117.2 78.6 %all-reduce.8.cloned.1.call-done = (f32[513,256]{1,0:T(8,128)}, f32[34,1024]{1,0:T(8,128)}) async-done(((f32[513,256]{1,0:T(8,128)}, f32[34,1024]{1,0:T(8,128)}), (f32[513,256]{1,0:T(8,128)}, f32[34,1024]{1,0:T(8,128)})) %all-reduce.8.cloned.1.call-update) | async-done | bytes 664592 | tf_op jit(solution)/shard_map/psum | solution.py:92
  197.8 1.6 slice_subtract_fusion
  201.4 1.9 fusion.88
  204.4 1.4 maximum_bitcast_fusion.1
  206.4 2.5 abs_reduce_fusion
  209.2 1.4 fusion.32
  210.7 1.4 fusion.38
  212.1 1.5 multiply_add_fusion.2
  213.6 1.4 fusion.50
  215.0 1.4 fusion.56
  216.4 1.5 fusion.62
  217.9 1.7 fusion.83
  219.6 6.2 %convolution_bitcast_fusion = f32[32,1,2,8192]{3,0,2,1:T(8,128)S(1)} fusion(bf16[8192,1024]{1,0:T(8,128)(2,1)} %param.8, bf16[2,2,32,512]{3,2,1,0:T(8,128)(2,1)S(1)} %fusion.83), kind=kOutput, calls=%fused_computation.1 | convolution fusion | flops 536870912 | bytes 10551296 | tf_op jit(solution)/shard_map/si,rpi->prs/dot_general | solution.py:148
  225.8 2.6 convolution_bitcast_fusion.1
  229.3 3.5 %copy.146 = bf16[32,2,2,8192]{3,2,1,0:T(2,128)(2,1)} copy(bf16[32,2,2,8192]{3,0,2,1:T(8,128)(2,1)S(1)} %fusion.8) | data formatting | bytes 4194304 | tf_op jit(solution)/shard_map/convert_element_type | solution.py:158
  232.8 4.4 %all-to-all-start = ((bf16[32,2,2,8192]{3,2,1,0:T(2,128)(2,1)}), bf16[32,2,2,8192]{3,2,1,0:T(2,128)(2,1)S(1)}, u32[]{:S(2)}, u32[]{:S(2)}) async-start(bf16[32,2,2,8192]{3,2,1,0:T(2,128)(2,1)} %copy.146), calls=%async_computation | async-start | bytes 4194304 | tf_op jit(solution)/shard_map/all_to_all | solution.py:159
  237.3 27.1 %all-to-all-done = bf16[32,2,2,8192]{3,2,1,0:T(2,128)(2,1)S(1)} async-done(((bf16[32,2,2,8192]{3,2,1,0:T(2,128)(2,1)}), bf16[32,2,2,8192]{3,2,1,0:T(2,128)(2,1)S(1)}, u32[]{:S(2)}, u32[]{:S(2)}) %all-to-all-start) | async-done | bytes 2097184 | tf_op jit(solution)/shard_map/all_to_all | solution.py:159
  264.4 3.2 copy.174
  267.6 2.7 reshape.893
  272.9 3.3 %collective-permute-done = f32[4,32,33]{2,1,0:T(8,128)S(1)} collective-permute-done((f32[4,32,33]{2,1,0:T(8,128)S(1)}, f32[4,32,33]{2,1,0:T(8,128)S(1)}, u32[]{:S(2)}, u32[]{:S(2)}) %collective-permute-start) | collective-permute-done | bytes 16928 | tf_op jit(solution)/shard_map/ppermute | solution.py:40
  276.3 1.8 collective-permute-start.1
  278.1 4.0 %collective-permute-done.1 = f32[4,32,33]{2,1,0:T(8,128)S(1)} collective-permute-done((f32[4,32,33]{2,1,0:T(8,128)S(1)}, f32[4,32,33]{2,1,0:T(8,128)S(1)}, u32[]{:S(2)}, u32[]{:S(2)}) %collective-permute-start.1) | collective-permute-done | bytes 16928 | tf_op jit(solution)/shard_map/ppermute | solution.py:40
  283.2 3.5 %collective-permute-done.2 = f32[4,32,33]{2,1,0:T(8,128)S(1)} collective-permute-done((f32[4,32,33]{2,1,0:T(8,128)S(1)}, f32[4,32,33]{2,1,0:T(8,128)S(1)}, u32[]{:S(2)}, u32[]{:S(2)}) %collective-permute-start.2) | collective-permute-done | bytes 16928 | tf_op jit(solution)/shard_map/ppermute | solution.py:40
  286.7 1.9 collective-permute-start.3
  288.6 4.0 %collective-permute-done.3 = f32[4,32,33]{2,1,0:T(8,128)S(1)} collective-permute-done((f32[4,32,33]{2,1,0:T(8,128)S(1)}, f32[4,32,33]{2,1,0:T(8,128)S(1)}, u32[]{:S(2)}, u32[]{:S(2)}) %collective-permute-start.3) | collective-permute-done | bytes 16928 | tf_op jit(solution)/shard_map/ppermute | solution.py:40
  293.0 11.7 %custom-call.11 = f32[4,32,32]{2,1,0:T(8,128)S(1)} custom-call(f32[4,32,32]{2,1,0:T(8,128)S(1)} %fusion.116), custom_call_target="Cholesky" | custom-call | tf_op jit(solution)/shard_map/jit(cholesky)/cholesky | solution.py:180
  305.0 9.8 %custom-call.12 = f32[4,1,32,32]{2,3,1,0:T(8,128)S(1)} custom-call(f32[4,1,32,32]{3,2,1,0:T(8,128)S(1)} %select_bitcast_fusion), custom_call_target="InvertDiagBlocksLowerTriangular" | custom-call | tf_op jit(solution)/shard_map/jit(_cho_solve)/vmap()/triangular_solve | solution.py:181
  (130 shorter events, 28.7 us)
Async XLA Ops:
  6.5 24.6 %copy-start = (bf16[32,8192]{1,0:T(8,128)(2,1)S(1)}, bf16[32,8192]{1,0:T(8,128)(2,1)}, u32[]{:S(2)}) copy-start(bf16[32,8192]{1,0:T(8,128)(2,1)} %param.9) | copy-start | bytes 1572868
  6.5 100.8 %all-reduce.6.cloned.1.call-start = ((), (), s32[]{:S(2)}) async-start(), calls=%async_computation.1 | async-start | bytes 1064960 | tf_op jit(solution)/shard_map/psum | solution.py:83
  16.4 1.0 copy-start.2
  17.9 2.1 copy-start.14
  19.2 176.5 %all-reduce.8.cloned.1.call-start = ((), (), s32[]{:S(2)}) async-start(), calls=%async_computation.2 | async-start | bytes 1392640 | tf_op jit(solution)/shard_map/psum | solution.py:92
  30.0 1.0 copy-start.4
  107.3 8.2 %copy-start.7 = (f32[513,256]{1,0:T(8,128)S(1)}, f32[513,256]{1,0:T(8,128)}, u32[]{:S(2)}) copy-start(f32[513,256]{1,0:T(8,128)} %all-reduce.6.cloned.1.call-done) | copy-start | bytes 1575940
  107.3 8.2 %slice-start.4 = ((f32[513,256]{1,0:T(8,128)}), f32[1,256]{1,0:T(1,128)S(1)}, s32[]{:S(2)}) async-start(f32[513,256]{1,0:T(8,128)} %all-reduce.6.cloned.1.call-done), calls=%async_computation.7 | async-start | bytes 2048 | tf_op jit(solution)/shard_map/slice | solution.py:65
  110.3 0.8 copy-start.6
  117.2 88.6 %copy-start.1 = (f32[1,512,512]{2,1,0:T(8,128)}, f32[1,512,512]{2,1,0:T(8,128)S(1)}, u32[]{:S(2)}) copy-start(f32[1,512,512]{2,1,0:T(8,128)S(1)} %copy.144) | copy-start | bytes 3145732
  195.7 5.6 %copy-start.8 = (f32[513,256]{1,0:T(8,128)S(1)}, f32[513,256]{1,0:T(8,128)}, u32[]{:S(2)}) copy-start(f32[513,256]{1,0:T(8,128)} %get-tuple-element.32) | copy-start | bytes 1575940
  201.4 4.4 %copy-start.9 = (pred[512,512]{1,0:T(8,128)(4,1)S(1)}, pred[512,512]{1,0:T(8,128)(4,1)}, u32[]{:S(2)}) copy-start(pred[512,512]{1,0:T(8,128)(4,1)} %iota_compare_fusion) | copy-start | bytes 786436
  204.4 1.9 copy-start.10
  204.4 1.8 copy-start.12
  204.4 1.9 copy-start.3
  204.4 1.9 copy-start.5
  206.4 2.7 copy-start.11
  206.4 2.7 copy-start.13
  209.2 16.6 %slice-start = ((s8[16777216]{0:T(1024)(128)(4,1)}), s8[4194304]{0:T(1024)(128)(4,1)S(1)}, s32[]{:S(2)}) async-start(s8[16777216]{0:T(1024)(128)(4,1)} %bitcast.178), calls=%async_computation.3 | async-start | bytes 8388608
  212.1 13.7 %slice-start.1 = ((s8[16777216]{0:T(1024)(128)(4,1)}), s8[4194304]{0:T(1024)(128)(4,1)S(1)}, s32[]{:S(2)}) async-start(s8[16777216]{0:T(1024)(128)(4,1)} %bitcast.178), calls=%async_computation.4 | async-start | bytes 8388608
  216.4 9.4 %slice-start.2 = ((s8[16777216]{0:T(1024)(128)(4,1)}), s8[4194304]{0:T(1024)(128)(4,1)S(1)}, s32[]{:S(2)}) async-start(s8[16777216]{0:T(1024)(128)(4,1)} %bitcast.178), calls=%async_computation.5 | async-start | bytes 8388608
  219.6 6.3 %slice-start.3 = ((s8[16777216]{0:T(1024)(128)(4,1)}), s8[4194304]{0:T(1024)(128)(4,1)S(1)}, s32[]{:S(2)}) async-start(s8[16777216]{0:T(1024)(128)(4,1)} %bitcast.178), calls=%async_computation.6 | async-start | bytes 8388608
  232.8 31.6 %all-to-all-start = ((bf16[32,2,2,8192]{3,2,1,0:T(2,128)(2,1)}), bf16[32,2,2,8192]{3,2,1,0:T(2,128)(2,1)S(1)}, u32[]{:S(2)}, u32[]{:S(2)}) async-start(bf16[32,2,2,8192]{3,2,1,0:T(2,128)(2,1)} %copy.146), calls=%async_computation | async-start | bytes 4194304 | tf_op jit(solution)/shard_map/all_to_all | solution.py:159
  271.9 4.3 %collective-permute-start = (f32[4,32,33]{2,1,0:T(8,128)S(1)}, f32[4,32,33]{2,1,0:T(8,128)S(1)}, u32[]{:S(2)}, u32[]{:S(2)}) collective-permute-start(f32[4,32,33]{2,1,0:T(8,128)S(1)} %pad_maximum_fusion.3), channel_id=1, source_target_pairs={{0,8},{8,0},{16,24},{24,16},{32,40},{40,32},{48,56},{56,48},{64,72... | collective-permute-start | bytes 50696 | tf_op jit(solution)/shard_map/ppermute | solution.py:40
  276.3 5.8 %collective-permute-start.1 = (f32[4,32,33]{2,1,0:T(8,128)S(1)}, f32[4,32,33]{2,1,0:T(8,128)S(1)}, u32[]{:S(2)}, u32[]{:S(2)}) collective-permute-start(f32[4,32,33]{2,1,0:T(8,128)S(1)} %fusion.151), channel_id=1, source_target_pairs={{0,16},{8,24},{16,0},{24,8},{32,48},{40,56},{48,32},{56,40},{64,80... | collective-permute-start | bytes 50696 | tf_op jit(solution)/shard_map/ppermute | solution.py:40
  282.2 4.5 %collective-permute-start.2 = (f32[4,32,33]{2,1,0:T(8,128)S(1)}, f32[4,32,33]{2,1,0:T(8,128)S(1)}, u32[]{:S(2)}, u32[]{:S(2)}) collective-permute-start(f32[4,32,33]{2,1,0:T(8,128)S(1)} %add.281), channel_id=1, source_target_pairs={{0,32},{8,40},{16,48},{24,56},{32,0},{40,8},{48,16},{56,24},{64,96... | collective-permute-start | bytes 50696 | tf_op jit(solution)/shard_map/ppermute | solution.py:40
  286.7 5.8 %collective-permute-start.3 = (f32[4,32,33]{2,1,0:T(8,128)S(1)}, f32[4,32,33]{2,1,0:T(8,128)S(1)}, u32[]{:S(2)}, u32[]{:S(2)}) collective-permute-start(f32[4,32,33]{2,1,0:T(8,128)S(1)} %add.282), channel_id=1, source_target_pairs={{0,64},{8,72},{16,80},{24,88},{32,96},{40,104},{48,112},{56,120},{... | collective-permute-start | bytes 50696 | tf_op jit(solution)/shard_map/ppermute | solution.py:40
Sparse Core Ops, SparseCore 0:
  19.3 87.9 all-reduce.5
  111.2 84.4 all-reduce.7

commit v3 on v2

--- a/solution.py
+++ b/solution.py
@@ -42,6 +42,24 @@
     return x
 
 
+def exchange_sum(arrays, axis):
+    n = lax.axis_size(axis)
+    flat = jnp.concatenate([a.reshape(-1) for a in arrays])
+    size = flat.shape[0]
+    unit = n * 8 * 128
+    flat = jnp.pad(flat, (0, -(-size // unit) * unit - size))
+    pieces = lax.all_to_all(flat.reshape(n, -1, 128), axis, 0, 0, tiled=True)
+    chunk = jnp.sum(pieces, axis=0)
+    whole = lax.all_to_all(jnp.broadcast_to(chunk[None], (n,) + chunk.shape), axis, 0, 0, tiled=True)
+    whole = whole.reshape(-1)
+    out = []
+    offset = 0
+    for a in arrays:
+        out.append(whole[offset:offset + a.size].reshape(a.shape))
+        offset += a.size
+    return out
+
+
 def per_device(genotypes, phenotypes, trait_order):
     n_fold = lax.axis_size("fold")
     sample_rows = genotypes.shape[0]
@@ -71,28 +89,18 @@
         return jnp.concatenate([top, bottom], axis=0)
 
     gram_parts = []
-    packed_sums = []
     for b in range(block_count):
         xb = genotypes[:, b * B:(b + 1) * B]
-        gram_b = jnp.einsum("si,sj->ij", xb, xb, preferred_element_type=jnp.float32)
-        gram_parts.append(gram_b)
-        if b + 1 < block_count:
-            packed = pack(gram_b)
-            if packed_sums:
-                packed = packed.at[0, 0].add(packed_sums[-1][0, 0] * 0.0)
-            packed_sums.append(lax.psum(packed, "fold"))
+        gram_parts.append(jnp.einsum("si,sj->ij", xb, xb, preferred_element_type=jnp.float32))
     phen_aug = jnp.concatenate([phen, jnp.ones((1, sample_rows), phen.dtype)], axis=0)
     cross_aug = jnp.dot(phen_aug, genotypes, preferred_element_type=jnp.float32)
     phen_local = jnp.sum(phen.astype(jnp.float32), axis=1)
     phen_row = jnp.zeros((1, genotypes.shape[1]), jnp.float32).at[0, :p_size].set(phen_local)
     sums_local = jnp.concatenate([cross_aug, phen_row], axis=0)
-    last_packed = pack(gram_parts[-1])
-    if packed_sums:
-        last_packed = last_packed.at[0, 0].add(packed_sums[-1][0, 0] * 0.0)
-    last_packed, sums_total = lax.psum((last_packed, sums_local), "fold")
-    packed_sums.append(last_packed)
+    totals = exchange_sum([pack(g) for g in gram_parts] + [sums_local], "fold")
+    sums_total = totals[-1]
     gram_part = jnp.stack(gram_parts)
-    gram_sum = jnp.stack([unpack(p) for p in packed_sums])
+    gram_sum = jnp.stack([unpack(p) for p in totals[:-1]])
     phen_total = sums_total[p_size + 1, :p_size]
     cross_aug = cross_aug.reshape(p_size + 1, block_count, B)
     cross_aug_total = sums_total[: p_size + 1].reshape(p_size + 1, block_count, B)

time: 324 us -> 225 us (0.69)
  waiting for transfers between devices: 184 us -> 60.3 us
  blocking collectives: 0 us -> 26.8 us
  between operations: 15.4 us -> 0.58 us
  local copies, waits for them, and re-layouts: 26 us -> 39.5 us
  matrix products: 50.9 us -> 45.6 us
  other arithmetic: 37.6 us -> 40.9 us
    psum x2 -> x0, waiting for transfers between devices: 142 us -> none  [the longest x1 78.6 us: per_device(): last_packed, sums_total = lax.psum((last_packed, sums_local), 'fold')]
    all_to_all x0 -> x1, blocking collectives: none -> 26.8 us  [exchange_sum(): pieces = lax.all_to_all(flat.reshape(n, -1, 128), axis, 0, 0, tiled=True)]
    all_to_all x0 -> x1, waiting for transfers between devices: none -> 15.1 us  [exchange_sum(): lax.all_to_all(jnp.broadcast_to(chunk[None], (n,) + chunk.shape), axis, 0...]
    dot_general x2, matrix products: 19.9 us -> 14.4 us  [per_device(): jnp.einsum('si,sj->ij', xb, xb, preferred_element_type=jnp.float32)]
    unnamed x45 -> x41, local copies, waits for them, and re-layouts: 3.2 us -> 7.74 us
    all_to_all x0 -> x1, starting transfers between devices: none -> 3.89 us  [exchange_sum(): lax.all_to_all(jnp.broadcast_to(chunk[None], (n,) + chunk.shape), axis, 0...]
    ppermute x4, starting transfers between devices: 5.77 us -> 2.43 us  [butterfly_sum(): x = x + lax.ppermute(x, axis, perm)]
  transfers between devices with their start and end apart: 7 -> 6, of which waited for: 7 -> 6; matrix products, arithmetic and copies ran while one was open for 9% -> 1% of each run, Pallas kernels for 0% -> 0%
where the time goes in v3:
time: 225 us; the launch traced here: 224 us
  waiting for transfers between devices  60.3 us (27%)
  matrix products  45.6 us (20%)
  other arithmetic  40.9 us (18%)
  local copies, waits for them, and re-layouts  39.5 us (18%)
  blocking collectives  26.8 us (12%)
  starting transfers between devices  10.8 us (5%)
    all_to_all x1, waiting for transfers between devices, per_device(): lax.all_to_all(feature, 'blk', split_axis=0, concat_axis=1, tiled=True)  27.1 us
    all_to_all x1, blocking collectives, exchange_sum(): pieces = lax.all_to_all(flat.reshape(n, -1, 128), axis, 0, 0, tiled=True)  26.8 us
    ppermute x4, waiting for transfers between devices, butterfly_sum(): x = x + lax.ppermute(x, axis, perm)  18 us
    all_to_all x1, waiting for transfers between devices, exchange_sum(): lax.all_to_all(jnp.broadcast_to(chunk[None], (n,) + chunk.shape), axis, 0...  15.1 us
    dot_general x2, matrix products, per_device(): jnp.einsum('si,sj->ij', xb, xb, preferred_element_type=jnp.float32)  14.4 us
    another operation x4, other arithmetic, per_device(): factor = jnp.linalg.cholesky(level_system)  11.9 us
    dot_general x7, matrix products, times_system(): jnp.einsum('brpi,bij->brpj', direction, system, precision=lax.Precision.H...  10.3 us
    another operation x3, other arithmetic, per_device(): jax.scipy.linalg.cho_solve((factor, True), (hcross_out / held_rows)[:, :,...  9.94 us
  transfers between devices with their start and end apart: 6, of which 6 were waited for; matrix products, arithmetic and copies ran while one was open for 1% of the time, Pallas kernels for 0%

profile of v3, /device:TPU:0, one launch (start us, length us, event | category | flops | bytes accessed | tf_op | source)
XLA Modules:
  0.0 224.5 jit_solution(745591110447071177)
XLA Ops:
  2.0 9.9 %fusion.6 = f32[512,512]{1,0:T(8,128)S(1)} fusion(bf16[8192,1024]{1,0:T(8,128)(2,1)} %param.6), kind=kOutput, calls=%fused_computation.9 | convolution fusion | flops 4294967296 | bytes 9437184 | tf_op jit(solution)/shard_map/si,sj->ij/dot_general | solution.py:94
  12.6 4.5 %fusion.3 = f32[512,512]{1,0:T(8,128)S(1)} fusion(bf16[8192,1024]{1,0:T(8,128)(2,1)S(1)} %copy-done.1), kind=kOutput, calls=%fused_computation.6 | convolution fusion | flops 4294967296 | bytes 9437184 | tf_op jit(solution)/shard_map/si,sj->ij/dot_general | solution.py:94
  17.2 1.7 gather_fusion
  20.2 8.7 %fusion.86 = f32[33,1024]{1,0:T(8,128)S(1)} fusion(bf16[8192,1024]{1,0:T(8,128)(2,1)} %param.6, bf16[32,8192]{1,0:T(8,128)(2,1)S(1)} %get-tuple-element.20), kind=kOutput, calls=%fused_computation.68 | convolution fusion | flops 553648128 | bytes 17436672 | tf_op jit(solution)/shard_map/dot_general | solution.py:96
  37.4 1.9 reshape.844
  40.9 26.8 %all_to_all.25 = f32[16,152,128]{2,1,0:T(8,128)S(1)} all-to-all(f32[16,152,128]{2,1,0:T(8,128)S(1)} %bitcast.187), channel_id=1, replica_groups=mesh['fold'=16,'blk'=8] {'fold'}, dimensions={0} | all-to-all | bytes 2490368 | tf_op jit(solution)/shard_map/all_to_all | solution.py:51
  68.9 3.9 %all-to-all-start.1 = ((f32[16,152,128]{2,1,0:T(8,128)}), f32[16,152,128]{2,1,0:T(8,128)S(1)}, u32[]{:S(2)}, u32[]{:S(2)}) async-start(f32[16,152,128]{2,1,0:T(8,128)} %broadcast_in_dim.110), calls=%async_computation.1 | async-start | bytes 2490368 | tf_op jit(solution)/shard_map/all_to_all | solution.py:53
  76.0 15.1 %all-to-all-done.1 = f32[16,152,128]{2,1,0:T(8,128)S(1)} async-done(((f32[16,152,128]{2,1,0:T(8,128)}), f32[16,152,128]{2,1,0:T(8,128)S(1)}, u32[]{:S(2)}, u32[]{:S(2)}) %all-to-all-start.1) | async-done | bytes 1245216 | tf_op jit(solution)/shard_map/all_to_all | solution.py:53
  93.9 1.8 copy.136
  95.7 2.5 %fusion.88 = (f32[256,256]{1,0:T(8,128)}, f32[256,256]{1,0:T(8,128)}, f32[256,256]{1,0:T(8,128)}, f32[256,256]{0,1:T(8,128)}, f32[256,256]{1,0:T(8,128)}, /*index=5*/f32[256,256]{0,1:T(8,128)}, f32[256,256]{1,0:T(8,128)}) fusion(pred[256,256]{1,0:T(8,128)(4,1)} %copy.139, pred[256,256]{1,0:T(8,128)(4,1)} %copy.137, f32[256,256]{1,0:T(8,128)} %copy.138, ...), kind=kLoop, calls=%fused_computation.73 | loop fusion | flops 196608 | bytes 3604480 | tf_op jit(solution)/shard_map/jit(_where)/select_n | solution.py:86
  98.2 1.8 copy.135
  99.9 1.8 copy.166
  102.7 2.1 maximum_bitcast_fusion
  104.8 1.6 copy.142
  106.4 2.0 copy.141
  113.2 3.1 %abs_reduce_fusion = (f32[2,512]{1,0:T(2,128)S(1)}, f32[2,512,512]{2,1,0:T(8,128)S(1)}) fusion(f32[2,512]{1,0:T(2,128)S(1)} %get-tuple-element.26, f32[2,512]{1,0:T(2,128)S(1)} %get-tuple-element.28, f32[2,512]{1,0:T(2,128)S(1)} %get-tuple-element.27, f32[2,512]{1,0:T(2,128)S(1)} %get-tuple-element.29, f32[1,512,512]{2,1,0:T(8,128)} %bitcast.189, ...), kind=kLoop, calls=%fused_computation.36 | loop fusion | flops 7339008 | bytes 6311936 | tf_op jit(solution)/shard_map/reduce_sum | solution.py:131
  119.5 1.5 multiply_add_fusion.2
  123.8 1.5 fusion.62
  125.3 1.7 fusion.83
  127.0 6.2 %convolution_bitcast_fusion = f32[32,1,2,8192]{3,0,2,1:T(8,128)S(1)} fusion(bf16[8192,1024]{1,0:T(8,128)(2,1)} %param.6, bf16[2,2,32,512]{3,2,1,0:T(8,128)(2,1)S(1)} %fusion.83), kind=kOutput, calls=%fused_computation.1 | convolution fusion | flops 536870912 | bytes 10551296 | tf_op jit(solution)/shard_map/si,rpi->prs/dot_general | solution.py:156
  133.2 2.7 %convolution_bitcast_fusion.1 = f32[32,1,2,8192]{3,0,2,1:T(8,128)S(1)} fusion(bf16[8192,1024]{1,0:T(8,128)(2,1)S(1)} %bitcast.181, bf16[2,2,32,512]{3,2,1,0:T(8,128)(2,1)S(1)} %fusion.83), kind=kOutput, calls=%fused_computation.2 | convolution fusion | flops 536870912 | bytes 10551296 | tf_op jit(solution)/shard_map/si,rpi->prs/dot_general | solution.py:156
  136.9 3.5 %copy.145 = bf16[32,2,2,8192]{3,2,1,0:T(2,128)(2,1)} copy(bf16[32,2,2,8192]{3,0,2,1:T(8,128)(2,1)S(1)} %fusion.8) | data formatting | bytes 4194304 | tf_op jit(solution)/shard_map/convert_element_type | solution.py:166
  140.4 4.5 %all-to-all-start.2 = ((bf16[32,2,2,8192]{3,2,1,0:T(2,128)(2,1)}), bf16[32,2,2,8192]{3,2,1,0:T(2,128)(2,1)S(1)}, u32[]{:S(2)}, u32[]{:S(2)}) async-start(bf16[32,2,2,8192]{3,2,1,0:T(2,128)(2,1)} %copy.145), calls=%async_computation.2 | async-start | bytes 4194304 | tf_op jit(solution)/shard_map/all_to_all | solution.py:167
  144.9 27.1 %all-to-all-done.2 = bf16[32,2,2,8192]{3,2,1,0:T(2,128)(2,1)S(1)} async-done(((bf16[32,2,2,8192]{3,2,1,0:T(2,128)(2,1)}), bf16[32,2,2,8192]{3,2,1,0:T(2,128)(2,1)S(1)}, u32[]{:S(2)}, u32[]{:S(2)}) %all-to-all-start.2) | async-done | bytes 2097184 | tf_op jit(solution)/shard_map/all_to_all | solution.py:167
  172.0 3.2 %copy.176 = bf16[8,4,2,2,8192]{4,3,2,0,1:T(2,128)(2,1)} copy(bf16[8,4,2,2,8192]{4,3,2,1,0:T(2,128)(2,1)S(1)} %bitcast.185) | data formatting | bytes 4194304 | tf_op jit(solution)/shard_map/all_to_all | solution.py:167
  175.2 2.7 %reshape.851 = bf16[4,32,8192]{2,1,0:T(8,128)(2,1)S(1)} reshape(bf16[4,8,2,2,8192]{4,3,2,1,0:T(2,128)(2,1)} %bitcast.186) | data formatting | bytes 4194304 | tf_op jit(solution)/shard_map/reshape | solution.py:170
  180.1 3.7 %collective-permute-done = f32[4,32,33]{2,1,0:T(8,128)S(1)} collective-permute-done((f32[4,32,33]{2,1,0:T(8,128)S(1)}, f32[4,32,33]{2,1,0:T(8,128)S(1)}, u32[]{:S(2)}, u32[]{:S(2)}) %collective-permute-start) | collective-permute-done | bytes 16928 | tf_op jit(solution)/shard_map/ppermute | solution.py:40
  185.0 4.8 %collective-permute-done.1 = f32[4,32,33]{2,1,0:T(8,128)S(1)} collective-permute-done((f32[4,32,33]{2,1,0:T(8,128)S(1)}, f32[4,32,33]{2,1,0:T(8,128)S(1)}, u32[]{:S(2)}, u32[]{:S(2)}) %collective-permute-start.1) | collective-permute-done | bytes 16928 | tf_op jit(solution)/shard_map/ppermute | solution.py:40
  189.9 4.3 %collective-permute-done.2 = f32[4,32,33]{2,1,0:T(8,128)S(1)} collective-permute-done((f32[4,32,33]{2,1,0:T(8,128)S(1)}, f32[4,32,33]{2,1,0:T(8,128)S(1)}, u32[]{:S(2)}, u32[]{:S(2)}) %collective-permute-start.2) | collective-permute-done | bytes 16928 | tf_op jit(solution)/shard_map/ppermute | solution.py:40
  194.8 5.2 %collective-permute-done.3 = f32[4,32,33]{2,1,0:T(8,128)S(1)} collective-permute-done((f32[4,32,33]{2,1,0:T(8,128)S(1)}, f32[4,32,33]{2,1,0:T(8,128)S(1)}, u32[]{:S(2)}, u32[]{:S(2)}) %collective-permute-start.3) | collective-permute-done | bytes 16928 | tf_op jit(solution)/shard_map/ppermute | solution.py:40
  200.5 11.7 %custom-call.11 = f32[4,32,32]{2,1,0:T(8,128)S(1)} custom-call(f32[4,32,32]{2,1,0:T(8,128)S(1)} %fusion.117), custom_call_target="Cholesky" | custom-call | tf_op jit(solution)/shard_map/jit(cholesky)/cholesky | solution.py:188
  212.5 9.8 %custom-call.12 = f32[4,1,32,32]{2,3,1,0:T(8,128)S(1)} custom-call(f32[4,1,32,32]{3,2,1,0:T(8,128)S(1)} %select_bitcast_fusion), custom_call_target="InvertDiagBlocksLowerTriangular" | custom-call | tf_op jit(solution)/shard_map/jit(_cho_solve)/vmap()/triangular_solve | solution.py:189
  (128 shorter events, 40.7 us)
Async XLA Ops:
  0.0 17.2 %copy-start = (bf16[32,8192]{1,0:T(8,128)(2,1)S(1)}, bf16[32,8192]{1,0:T(8,128)(2,1)}, u32[]{:S(2)}) copy-start(bf16[32,8192]{1,0:T(8,128)(2,1)} %param.7) | copy-start | bytes 1572868
  2.0 10.6 %copy-start.1 = (bf16[8192,1024]{1,0:T(8,128)(2,1)S(1)}, bf16[8192,1024]{1,0:T(8,128)(2,1)}, u32[]{:S(2)}) copy-start(bf16[8192,1024]{1,0:T(8,128)(2,1)} %param.6) | copy-start | bytes 50331652
  12.6 17.7 %copy-start.4 = (f32[512,512]{1,0:T(8,128)}, f32[512,512]{1,0:T(8,128)S(1)}, u32[]{:S(2)}) copy-start(f32[512,512]{1,0:T(8,128)S(1)} %fusion.6) | copy-start | bytes 3145732
  17.1 22.1 %copy-start.5 = (f32[512,512]{1,0:T(8,128)}, f32[512,512]{1,0:T(8,128)S(1)}, u32[]{:S(2)}) copy-start(f32[512,512]{1,0:T(8,128)S(1)} %fusion.3) | copy-start | bytes 3145732
  28.9 46.3 %copy-start.7 = (f32[33,1024]{1,0:T(8,128)}, f32[33,1024]{1,0:T(8,128)S(1)}, u32[]{:S(2)}) copy-start(f32[33,1024]{1,0:T(8,128)S(1)} %fusion.86) | copy-start | bytes 405508
  39.7 1.0 copy-start.6
  39.7 1.1 copy-start.9
  68.9 22.3 %all-to-all-start.1 = ((f32[16,152,128]{2,1,0:T(8,128)}), f32[16,152,128]{2,1,0:T(8,128)S(1)}, u32[]{:S(2)}, u32[]{:S(2)}) async-start(f32[16,152,128]{2,1,0:T(8,128)} %broadcast_in_dim.110), calls=%async_computation.1 | async-start | bytes 2490368 | tf_op jit(solution)/shard_map/all_to_all | solution.py:53
  106.4 4.7 %copy-start.2 = (f32[1,512,512]{2,1,0:T(8,128)}, f32[1,512,512]{2,1,0:T(8,128)S(1)}, u32[]{:S(2)}) copy-start(f32[1,512,512]{2,1,0:T(8,128)S(1)} %copy.142) | copy-start | bytes 3145732
  108.4 2.3 %copy-start.8 = (pred[512,512]{1,0:T(8,128)(4,1)S(1)}, pred[512,512]{1,0:T(8,128)(4,1)}, u32[]{:S(2)}) copy-start(pred[512,512]{1,0:T(8,128)(4,1)} %iota_compare_fusion.1) | copy-start | bytes 786436
  109.7 1.0 copy-start.3
  113.1 3.3 %slice-start.4 = ((f32[33,1024]{1,0:T(8,128)}), f32[32,1024]{1,0:T(8,128)S(1)}, s32[]{:S(2)}) async-start(f32[33,1024]{1,0:T(8,128)} %copy-done.7), calls=%async_computation.7 | async-start | bytes 262144 | tf_op jit(solution)/shard_map/slice | solution.py:107
  113.1 3.3 %copy-start.10 = (f32[32,2,512]{2,1,0:T(2,128)S(1)}, f32[32,2,512]{2,1,0:T(2,128)}, u32[]{:S(2)}) copy-start(f32[32,2,512]{2,1,0:T(2,128)} %slice.164) | copy-start | bytes 393220
  113.1 3.3 %copy-start.11 = (f32[2]{0:T(128)S(1)}, f32[2]{0:T(128)}, u32[]{:S(2)}) copy-start(f32[2]{0:T(128)} %constant.145.clone) | copy-start | bytes 28
  113.1 3.3 %copy-start.12 = (f32[2]{0:T(128)S(1)}, f32[2]{0:T(128)}, u32[]{:S(2)}) copy-start(f32[2]{0:T(128)} %constant.152) | copy-start | bytes 28
  116.6 16.6 %slice-start = ((s8[16777216]{0:T(1024)(128)(4,1)}), s8[4194304]{0:T(1024)(128)(4,1)S(1)}, s32[]{:S(2)}) async-start(s8[16777216]{0:T(1024)(128)(4,1)} %bitcast.180), calls=%async_computation.3 | async-start | bytes 8388608
  119.5 13.7 %slice-start.1 = ((s8[16777216]{0:T(1024)(128)(4,1)}), s8[4194304]{0:T(1024)(128)(4,1)S(1)}, s32[]{:S(2)}) async-start(s8[16777216]{0:T(1024)(128)(4,1)} %bitcast.180), calls=%async_computation.4 | async-start | bytes 8388608
  123.8 9.4 %slice-start.2 = ((s8[16777216]{0:T(1024)(128)(4,1)}), s8[4194304]{0:T(1024)(128)(4,1)S(1)}, s32[]{:S(2)}) async-start(s8[16777216]{0:T(1024)(128)(4,1)} %bitcast.180), calls=%async_computation.5 | async-start | bytes 8388608
  127.0 6.2 %slice-start.3 = ((s8[16777216]{0:T(1024)(128)(4,1)}), s8[4194304]{0:T(1024)(128)(4,1)S(1)}, s32[]{:S(2)}) async-start(s8[16777216]{0:T(1024)(128)(4,1)} %bitcast.180), calls=%async_computation.6 | async-start | bytes 8388608
  140.4 31.6 %all-to-all-start.2 = ((bf16[32,2,2,8192]{3,2,1,0:T(2,128)(2,1)}), bf16[32,2,2,8192]{3,2,1,0:T(2,128)(2,1)S(1)}, u32[]{:S(2)}, u32[]{:S(2)}) async-start(bf16[32,2,2,8192]{3,2,1,0:T(2,128)(2,1)} %copy.145), calls=%async_computation.2 | async-start | bytes 4194304 | tf_op jit(solution)/shard_map/all_to_all | solution.py:167
  179.5 4.3 %collective-permute-start = (f32[4,32,33]{2,1,0:T(8,128)S(1)}, f32[4,32,33]{2,1,0:T(8,128)S(1)}, u32[]{:S(2)}, u32[]{:S(2)}) collective-permute-start(f32[4,32,33]{2,1,0:T(8,128)S(1)} %pad_maximum_fusion.3), channel_id=1, source_target_pairs={{0,8},{8,0},{16,24},{24,16},{32,40},{40,32},{48,56},{56,48},{64,72... | collective-permute-start | bytes 50696 | tf_op jit(solution)/shard_map/ppermute | solution.py:40
  183.9 5.8 %collective-permute-start.1 = (f32[4,32,33]{2,1,0:T(8,128)S(1)}, f32[4,32,33]{2,1,0:T(8,128)S(1)}, u32[]{:S(2)}, u32[]{:S(2)}) collective-permute-start(f32[4,32,33]{2,1,0:T(8,128)S(1)} %fusion.151), channel_id=1, source_target_pairs={{0,16},{8,24},{16,0},{24,8},{32,48},{40,56},{48,32},{56,40},{64,80... | collective-permute-start | bytes 50696 | tf_op jit(solution)/shard_map/ppermute | solution.py:40
  189.8 4.4 %collective-permute-start.2 = (f32[4,32,33]{2,1,0:T(8,128)S(1)}, f32[4,32,33]{2,1,0:T(8,128)S(1)}, u32[]{:S(2)}, u32[]{:S(2)}) collective-permute-start(f32[4,32,33]{2,1,0:T(8,128)S(1)} %add.257), channel_id=1, source_target_pairs={{0,32},{8,40},{16,48},{24,56},{32,0},{40,8},{48,16},{56,24},{64,96... | collective-permute-start | bytes 50696 | tf_op jit(solution)/shard_map/ppermute | solution.py:40
  194.2 5.8 %collective-permute-start.3 = (f32[4,32,33]{2,1,0:T(8,128)S(1)}, f32[4,32,33]{2,1,0:T(8,128)S(1)}, u32[]{:S(2)}, u32[]{:S(2)}) collective-permute-start(f32[4,32,33]{2,1,0:T(8,128)S(1)} %add.258), channel_id=1, source_target_pairs={{0,64},{8,72},{16,80},{24,88},{32,96},{40,104},{48,112},{56,120},{... | collective-permute-start | bytes 50696 | tf_op jit(solution)/shard_map/ppermute | solution.py:40
